TPU v7x, 32 devices: a whole 2x2x4 slice. The times are simulated.
32 devices in a mesh: space: 16 (over z, y, x), ray: 2 (over core).
Axes of the slice: x: 2, y: 2, z: 4, core: 2. Of those that a mesh axis runs over, the one named last changes fastest.
Arguments:
- positions: float32 [3, 512, 256], P(None, ('space', 'ray')), may hold values from -1 to 1
- spacing: float32 [512, 256], P(('space', 'ray')), may hold values from 0.003 to 0.03
- assign: int32 [512, 8, 1], P(('space', 'ray')), may hold values from 0 to 15; in each aligned block of 128 rows (0 to 127, 128 to 255, ..., all dimensions but the last counted through in order) at most 12 rows name the same one
- depth_rank: int32 [512, 8], P(('space', 'ray')), may hold values from 0 to 7, each once within a row
- pixel_grad: float32 [3, 512], P(None, ('space', 'ray')), may hold values from -96 to 96
- fourier: float32 [3, 128], replicated, may hold values from -4 to 4
- first_weight: bfloat16 [16, 256, 256], P('space'), may hold values from -0.375 to 0.375
- first_bias: float32 [16, 256], P('space'), may hold values from -3 to 3
- second_weight: bfloat16 [16, 256, 256], P('space'), may hold values from -0.375 to 0.375
- second_bias: float32 [16, 256], P('space'), may hold values from -3 to 3
- head_weight: bfloat16 [16, 4, 256], P('space'), may hold values from -0.375 to 0.375
- head_bias: float32 [16, 4], P('space'), may hold values from -3 to 3
Outputs:
- grad_first: float32 [16, 256, 256], P('space', 'ray')
- grad_second: float32 [16, 256, 256], P('space', 'ray')
- grad_head: float32 [16, 4, 256], P('space')
- grad_first_bias: float32 [16, 256], P('space')
- grad_second_bias: float32 [16, 256], P('space')
- grad_head_bias: float32 [16, 4], P('space')
Inputs may be any that keep to these rules, and one draw needn't show every extreme that they name: `assign`: within the segments of one device (aligned blocks of 128 rows in ray order), no partition is named more than 12 times. `depth_rank`: each ray's row names every place 0 to 7 once.
All inputs are finite; a program needn't handle non-finite values.
Results may differ from a plain program's by a relative error of at most 0.0053.
Values sent between devices are 32-bit elements; how exact they have to be, the bound alone decides.
No kernel may reach another device: no remote copies, remote signals or barrier semaphores. Data moves between devices by JAX's collectives and lax.ppermute only.
A program may use at most 64 MiB of HBM per device.

v0:
```python
import jax
import jax.numpy as jnp
from jax import lax
from jax.sharding import PartitionSpec as P

SEG_LEN = 32
SEGS = 8
two_pi = 6.283185307179586


def silu_slope(value):
    gate = jax.nn.sigmoid(value)
    return gate * (1.0 + value * (1.0 - gate))


def turn_sin_cos(turns):
    quarter = jnp.round(turns * 4.0)
    angle = (turns - quarter * 0.25) * two_pi
    square = angle * angle
    sine = angle * (
        1.0
        + square
        * (
            -1.0 / 6.0
            + square * (1.0 / 120.0 + square * (-1.0 / 5040.0 + square * (1.0 / 362880.0)))
        )
    )
    cosine = 1.0 + square * (
        -0.5
        + square
        * (
            1.0 / 24.0
            + square * (-1.0 / 720.0 + square * (1.0 / 40320.0 + square * (-1.0 / 3628800.0)))
        )
    )
    step = quarter - 4.0 * jnp.floor(quarter * 0.25)
    flip = step >= 2.0
    odd = (step == 1.0) | (step == 3.0)
    sin_out = jnp.where(odd, cosine, sine)
    cos_out = jnp.where(odd, sine, cosine)
    sin_out = jnp.where(flip, -sin_out, sin_out)
    cos_out = jnp.where(flip != odd, -cos_out, cos_out)
    return (sin_out, cos_out)


def encode(samples, fourier):
    turns = (
        samples[:, 0, :, None] * fourier[0]
        + samples[:, 1, :, None] * fourier[1]
        + samples[:, 2, :, None] * fourier[2]
    )
    sine, cosine = turn_sin_cos(turns)
    joined = jnp.concatenate([sine, cosine], axis=-1)
    return joined.astype(jnp.bfloat16).reshape(-1, joined.shape[-1])


def network(samples, fourier, params):
    first_weight, first_bias, second_weight, second_bias, head_weight, head_bias = params
    seg_count, length = (samples.shape[0], samples.shape[2])
    encoded = encode(samples, fourier)
    pre_first = jnp.dot(encoded, first_weight, preferred_element_type=jnp.float32) + first_bias
    act_first = jax.nn.silu(pre_first).astype(jnp.bfloat16)
    pre_second = jnp.dot(act_first, second_weight, preferred_element_type=jnp.float32) + second_bias
    act_second = jax.nn.silu(pre_second).astype(jnp.bfloat16)
    head_raw = (
        lax.dot_general(
            act_second, head_weight, (((1,), (1,)), ((), ())), preferred_element_type=jnp.float32
        )
        + head_bias
    )
    head_raw = head_raw.reshape(seg_count, length, 4)
    density = jax.nn.softplus(head_raw[..., 0])
    colour = jax.nn.sigmoid(head_raw[..., 1:])
    optical = density * samples[:, 3, :]
    inclusive = jnp.cumsum(optical, axis=1)
    enter_light = jnp.exp(optical - inclusive)
    leave_light = jnp.exp(-inclusive)
    weight = enter_light - leave_light
    seg_colour = jnp.sum(weight[..., None] * colour, axis=1)
    seg_log = -inclusive[:, -1]
    saved = (
        encoded,
        pre_first,
        act_first,
        pre_second,
        act_second,
        head_raw,
        colour,
        weight,
        leave_light,
    )
    return (seg_colour, seg_log, saved)


def backward(samples, params, saved, up_colour, up_log):
    first_weight, first_bias, second_weight, second_bias, head_weight, head_bias = params
    encoded, pre_first, act_first, pre_second, act_second, head_raw, colour, weight, leave_light = (
        saved
    )
    energy = jnp.sum(colour * up_colour[:, None, :], axis=-1)
    spent = weight * energy
    remaining = jnp.sum(spent, axis=1, keepdims=True) - jnp.cumsum(spent, axis=1)
    grad_optical = leave_light * energy - remaining - up_log[:, None]
    grad_density = grad_optical * samples[:, 3, :] * jax.nn.sigmoid(head_raw[..., 0])
    grad_tint = weight[..., None] * up_colour[:, None, :] * colour * (1.0 - colour)
    grad_raw = (
        jnp.concatenate([grad_density[..., None], grad_tint], axis=-1)
        .reshape(-1, 4)
        .astype(jnp.bfloat16)
    )
    grad_head = lax.dot_general(
        grad_raw, act_second, (((0,), (0,)), ((), ())), preferred_element_type=jnp.float32
    )
    grad_head_bias = jnp.sum(grad_raw.astype(jnp.float32), axis=0)
    back_second = jnp.dot(grad_raw, head_weight, preferred_element_type=jnp.float32)
    delta_second = (back_second * silu_slope(pre_second)).astype(jnp.bfloat16)
    grad_second = lax.dot_general(
        act_first, delta_second, (((0,), (0,)), ((), ())), preferred_element_type=jnp.float32
    )
    grad_second_bias = jnp.sum(delta_second.astype(jnp.float32), axis=0)
    back_first = lax.dot_general(
        delta_second, second_weight, (((1,), (1,)), ((), ())), preferred_element_type=jnp.float32
    )
    delta_first = (back_first * silu_slope(pre_first)).astype(jnp.bfloat16)
    grad_first = lax.dot_general(
        encoded, delta_first, (((0,), (0,)), ((), ())), preferred_element_type=jnp.float32
    )
    grad_first_bias = jnp.sum(delta_first.astype(jnp.float32), axis=0)
    return (grad_first, grad_second, grad_head, grad_first_bias, grad_second_bias, grad_head_bias)


def composite(seg_colour, seg_log, depth_rank, pixel_rows):
    before = (depth_rank[:, None, :] < depth_rank[:, :, None]).astype(jnp.float32)
    prefix = jnp.exp(jnp.sum(before * seg_log[:, None, :], axis=2))
    up_colour = prefix[..., None] * pixel_rows[:, None, :]
    shaded = prefix * jnp.sum(seg_colour * pixel_rows[:, None, :], axis=2)
    up_log = jnp.sum(before * shaded[:, :, None], axis=1)
    return (up_colour, up_log)


def per_device(
    positions,
    spacing,
    assign,
    depth_rank,
    pixel_grad,
    fourier,
    first_weight,
    first_bias,
    second_weight,
    second_bias,
    head_weight,
    head_bias,
):
    groups = lax.axis_size("space")
    ray_count = positions.shape[1]
    total = ray_count * SEGS
    capacity = 3 * total // (2 * groups)
    slot_count = capacity * groups
    owner = assign.reshape(total)
    member = (owner[:, None] == jnp.arange(groups, dtype=jnp.int32)[None, :]).astype(jnp.int32)
    earlier = jnp.cumsum(member, axis=0) - member
    within = jnp.sum(earlier * member, axis=1)
    target = owner * capacity + within
    dispatch = (target[:, None] == jnp.arange(slot_count, dtype=jnp.int32)[None, :]).astype(
        jnp.float32
    )
    seg_pos = jnp.transpose(positions.reshape(3, total, SEG_LEN), (1, 0, 2))
    seg_gap = spacing.reshape(total, 1, SEG_LEN)
    segments = jnp.concatenate([seg_pos, seg_gap], axis=1).reshape(total, 4 * SEG_LEN)
    outgoing = lax.dot_general(
        dispatch,
        segments,
        (((0,), (0,)), ((), ())),
        precision=lax.Precision.HIGHEST,
        preferred_element_type=jnp.float32,
    )
    outgoing = outgoing.reshape(groups, capacity, 4 * SEG_LEN)
    arrived = lax.all_to_all(outgoing, "space", split_axis=0, concat_axis=0, tiled=True)
    samples = arrived.reshape(slot_count, 4, SEG_LEN)
    params = tuple(
        (
            item[0]
            for item in (
                first_weight,
                first_bias,
                second_weight,
                second_bias,
                head_weight,
                head_bias,
            )
        )
    )
    seg_colour, seg_log, saved = network(samples, fourier, params)
    partials = jnp.concatenate([seg_colour.T, seg_log[None, :]], axis=0).reshape(
        4, groups, capacity
    )
    returned = lax.all_to_all(partials, "space", split_axis=1, concat_axis=1, tiled=True).reshape(
        4, slot_count
    )
    mine = lax.dot_general(
        dispatch,
        returned,
        (((1,), (1,)), ((), ())),
        precision=lax.Precision.HIGHEST,
        preferred_element_type=jnp.float32,
    )
    up_colour, up_log = composite(
        mine[:, :3].reshape(ray_count, SEGS, 3),
        mine[:, 3].reshape(ray_count, SEGS),
        depth_rank,
        pixel_grad.T,
    )
    upstream = jnp.concatenate([up_colour.reshape(total, 3), up_log.reshape(total, 1)], axis=1)
    sendback = lax.dot_general(
        upstream,
        dispatch,
        (((0,), (0,)), ((), ())),
        precision=lax.Precision.HIGHEST,
        preferred_element_type=jnp.float32,
    )
    sendback = sendback.reshape(4, groups, capacity)
    received = lax.all_to_all(sendback, "space", split_axis=1, concat_axis=1, tiled=True)
    received = received.reshape(4, slot_count).T
    totals = backward(samples, params, saved, received[:, :3], received[:, 3])
    grad_first, grad_second, grad_head, bias_first, bias_second, bias_head = totals
    replicas = lax.axis_size("ray")
    small = jnp.concatenate([grad_head.reshape(-1), bias_first, bias_second, bias_head], axis=0)
    if replicas & replicas - 1 == 0:
        position = lax.axis_index("ray")
        part_first, part_second = (grad_first, grad_second)
        distance = replicas // 2
        while distance >= 1:
            pairs = [(i, i ^ distance) for i in range(replicas)]
            half = part_first.shape[0] // 2
            upper = position // distance % 2
            keep_first = lax.dynamic_slice_in_dim(part_first, upper * half, half, 0)
            send_first = lax.dynamic_slice_in_dim(part_first, (1 - upper) * half, half, 0)
            keep_second = lax.dynamic_slice_in_dim(part_second, upper * half, half, 0)
            send_second = lax.dynamic_slice_in_dim(part_second, (1 - upper) * half, half, 0)
            got_first, got_second, got_small = lax.ppermute(
                (send_first, send_second, small), "ray", pairs
            )
            part_first = keep_first + got_first
            part_second = keep_second + got_second
            small = small + got_small
            distance //= 2
    else:
        part_first = lax.psum_scatter(grad_first, "ray", scatter_dimension=0, tiled=True)
        part_second = lax.psum_scatter(grad_second, "ray", scatter_dimension=0, tiled=True)
        small = lax.psum(small, "ray")
    heads = grad_head.size
    hidden = bias_first.shape[0]
    small_sums = (
        small[:heads].reshape(grad_head.shape),
        small[heads : heads + hidden],
        small[heads + hidden : heads + 2 * hidden],
        small[heads + 2 * hidden :],
    )
    return (
        part_first[None],
        part_second[None],
        small_sums[0][None],
        small_sums[1][None],
        small_sums[2][None],
        small_sums[3][None],
    )


def solution(mesh):
    placed = (
        P(None, ("space", "ray"), None),
        P(("space", "ray"), None),
        P(("space", "ray"), None, None),
        P(("space", "ray"), None),
        P(None, ("space", "ray")),
        P(),
        P("space", None, None),
        P("space", None),
        P("space", None, None),
        P("space", None),
        P("space", None, None),
        P("space", None),
    )
    return jax.shard_map(
        per_device,
        mesh=mesh,
        in_specs=placed,
        out_specs=(
            P("space", "ray", None),
            P("space", "ray", None),
            P("space", None, None),
            P("space", None),
            P("space", None),
            P("space", None),
        ),
        check_vma=False,
    )
```

profile of v0, /device:TPU:1, one launch (start us, length us, event | category | flops | bytes accessed | tf_op | source)
XLA Modules:
  0.0 90.0 jit_solution(858286756958283039)
XLA Ops:
  0.7 0.8 copy.53
  2.0 0.9 reshape.234
  3.0 0.8 reshape.235
  4.0 0.9 fusion.21
  4.9 7.4 %all-to-all-start = ((f32[16,12,128]{2,1,0:T(8,128)}), f32[16,12,128]{2,1,0:T(8,128)S(1)}, u32[]{:S(2)}, u32[]{:S(2)}) async-start(f32[16,12,128]{2,1,0:T(8,128)} %fusion.21), calls=%async_computation | async-start | bytes 262144 | tf_op jit(solution)/shard_map/all_to_all | solution.py:179
  12.3 0.8 slice_bitcast_fusion.3
  13.1 5.8 %all-to-all-done = f32[16,12,128]{2,1,0:T(8,128)S(1)} async-done(((f32[16,12,128]{2,1,0:T(8,128)}), f32[16,12,128]{2,1,0:T(8,128)S(1)}, u32[]{:S(2)}, u32[]{:S(2)}) %all-to-all-start) | async-done | bytes 98336 | tf_op jit(solution)/shard_map/all_to_all | solution.py:179
  19.2 0.9 %slice_reduce_fusion.2 = (f32[192,32]{1,0:T(8,128)S(1)}, f32[192,32]{1,0:T(8,128)S(1)}, f32[192,32]{1,0:T(8,128)S(1)}, f32[192,1,32]{2,1,0:T(1,128)S(1)}) fusion(f32[192,4,32]{2,1,0:T(4,128)S(1)} %reshape.237), kind=kLoop, calls=%fused_computation.61 | loop fusion | bytes 196608 | tf_op jit(solution)/shard_map/slice | solution.py:48
  20.4 5.6 %fusion.2 = (bf16[6144,128]{1,0:T(8,128)(2,1)S(1)}, bf16[6144,128]{1,0:T(8,128)(2,1)S(1)}) fusion(f32[128]{0:T(128)S(1)} %get-tuple-element.19, f32[6144]{0:T(1024)S(1)} %mul.319, f32[128]{0:T(128)S(1)} %get-tuple-element.20, f32[6144]{0:T(1024)S(1)} %mul.314, f32[128]{0:T(128)S(1)} %get-tuple-element.18, f32[6144]{0:T(1024)S(1)} %mul.309), kind=kLoop, calls=%fused_computation.15 | loop fusion | flops 36175872 | bytes 3220992 | tf_op jit(solution)/shard_map/convert.4
  26.1 4.7 %multiply_convert_fusion.1 = (bf16[6144,256]{1,0:T(8,128)(2,1)S(1)}, f32[6144,256]{1,0:T(8,128)}) fusion(f32[256]{0:T(256)S(1)} %bitcast.134, bf16[1,256,256]{2,1,0:T(8,128)(2,1)} %param.18, bf16[6144,128]{1,0:T(8,128)(2,1)S(1)} %get-tuple-element.13, bf16[6144,128]{1,0:T(8,128)(2,1)S(1)} %get-tuple-element.12), kind=kOutput, calls=%fused_computation.11 | convolution fusion | flops 821035008 | bytes 12715008 | tf_op jit(solution)/shard_map/dot_general | solution.py:61
  30.9 4.4 %multiply_convert_fusion = (bf16[6144,256]{1,0:T(8,128)(2,1)S(1)}, f32[6144,256]{1,0:T(8,128)}) fusion(f32[256]{0:T(256)S(1)} %bitcast.135, bf16[6144,256]{1,0:T(8,128)(2,1)S(1)} %get-tuple-element.21, bf16[1,256,256]{2,1,0:T(8,128)(2,1)S(1)} %copy-done), kind=kOutput, calls=%fused_computation.9 | convolution fusion | flops 814743552 | bytes 12715008 | tf_op jit(solution)/shard_map/dot_general | solution.py:63
  35.3 0.9 %convolution_add_fusion.2 = f32[6144,4]{0,1:T(4,128)S(1)} fusion(bf16[6144,256]{1,0:T(8,128)(2,1)S(1)} %get-tuple-element.23, f32[4]{0:T(128)S(1)} %bitcast.130, bf16[1,4,256]{2,1,0:T(4,128)(2,1)S(1)} %copy-done.6), kind=kOutput, calls=%fused_computation.6 | convolution fusion | flops 12607488 | bytes 3246096 | tf_op jit(solution)/shard_map/dot_general | solution.py:66
  36.2 0.9 %reshape.238 = f32[192,32,4]{1,0,2:T(8,128)} reshape(f32[6144,4]{0,1:T(4,128)S(1)} %convolution_add_fusion.2) | data formatting | bytes 196608 | tf_op jit(solution)/shard_map/reshape | solution.py:71
  37.1 0.9 slice.77
  38.4 1.2 %multiply_reduce_fusion.1 = f32[192,3]{0,1:T(4,128)S(1)} fusion(f32[192,32]{1,0:T(8,128)S(1)} %copy.60, f32[192,32,4]{1,0,2:T(8,128)} %reshape.238), kind=kLoop, calls=%fused_computation.48 | loop fusion | flops 91584 | bytes 100608 | tf_op jit(solution)/shard_map/reduce_sum | solution.py:79
  40.4 3.5 %all-to-all-start.1 = ((f32[4,16,12]{2,0,1:T(4,128)}), f32[4,16,12]{2,0,1:T(4,128)S(1)}, u32[]{:S(2)}, u32[]{:S(2)}) async-start(f32[4,16,12]{2,0,1:T(4,128)} %copy.61), calls=%async_computation.1 | async-start | bytes 65536 | tf_op jit(solution)/shard_map/all_to_all | solution.py:198
  44.6 0.8 mul.354
  45.4 4.7 %all-to-all-done.1 = f32[4,16,12]{2,0,1:T(4,128)S(1)} async-done(((f32[4,16,12]{2,0,1:T(4,128)}), f32[4,16,12]{2,0,1:T(4,128)S(1)}, u32[]{:S(2)}, u32[]{:S(2)}) %all-to-all-start.1) | async-done | bytes 3104 | tf_op jit(solution)/shard_map/all_to_all | solution.py:198
  50.8 0.8 reshape.239
  51.6 0.8 fusion.20
  53.3 0.9 fusion.19
  54.9 3.7 %all-to-all-start.2 = ((f32[4,16,12]{2,0,1:T(4,128)}), f32[4,16,12]{2,0,1:T(4,128)S(1)}, u32[]{:S(2)}, u32[]{:S(2)}) async-start(f32[4,16,12]{2,0,1:T(4,128)} %copy.67), calls=%async_computation.2 | async-start | bytes 65536 | tf_op jit(solution)/shard_map/all_to_all | solution.py:223
  58.6 6.0 %all-to-all-done.2 = f32[4,16,12]{2,0,1:T(4,128)S(1)} async-done(((f32[4,16,12]{2,0,1:T(4,128)}), f32[4,16,12]{2,0,1:T(4,128)S(1)}, u32[]{:S(2)}, u32[]{:S(2)}) %all-to-all-start.2) | async-done | bytes 3104 | tf_op jit(solution)/shard_map/all_to_all | solution.py:223
  65.2 0.8 reshape.242
  66.1 2.4 %multiply_reduce_fusion = (f32[192,32]{1,0:T(8,128)}, bf16[192,32,3]{1,0,2:T(8,128)(2,1)}) fusion(f32[192,3]{0,1:T(4,128)S(1)} %bitcast.126, f32[192,32,4]{1,0,2:T(8,128)} %reshape.238, f32[192,32]{1,0:T(8,128)S(1)} %copy.60), kind=kLoop, calls=%fused_computation.47 | loop fusion | flops 178176 | bytes 162048 | tf_op jit(solution)/shard_map/reduce_sum | solution.py:100
  68.5 1.0 %copy.69 = f32[192,32]{0,1:T(8,128)S(1)} copy(f32[192,32]{1,0:T(8,128)} %get-tuple-element.9) | data formatting | bytes 49152 | tf_op jit(solution)/shard_map/reduce_sum | solution.py:100
  69.9 1.1 %concatenate.35 = bf16[6144,3]{0,1:T(4,128)(2,1)S(1)} reshape(bf16[192,32,3]{1,0,2:T(8,128)(2,1)} %get-tuple-element.10) | data formatting | bytes 73728 | tf_op jit(solution)/shard_map/concatenate | solution.py:107
  71.7 5.2 %convert_reduce_fusion = (f32[256]{0:T(256)S(1)}, bf16[6144,256]{1,0:T(8,128)(2,1)S(1)}) fusion(f32[6144,256]{1,0:T(8,128)} %get-tuple-element.24, bf16[1,4,256]{2,1,0:T(4,128)(2,1)S(1)} %copy-done.6, bf16[6144,3]{0,1:T(4,128)(2,1)S(1)} %concatenate.35, bf16[6144,1]{0,1:T(2,128)(2,1)S(1)} %concatenate.34), kind=kOutput, calls=%fused_computation.7 | convolution fusion | flops 29982464 | bytes 9489408 | tf_op jit(solution)/shard_map/dot_general | solution.py:115
  76.9 1.0 %fusion.56 = f32[256,256]{1,0:T(8,128)S(1)} fusion(bf16[6144,256]{1,0:T(8,128)(2,1)S(1)} %copy-done.13, bf16[6144,256]{1,0:T(8,128)(2,1)S(1)} %get-tuple-element.26), kind=kOutput, calls=%fused_computation.126 | convolution fusion | flops 805306368 | bytes 6553600 | tf_op jit(solution)/shard_map/dot_general | solution.py:117
  78.0 2.8 %convert_reduce_fusion.1 = (f32[256]{0:T(256)S(1)}, bf16[6144,256]{1,0:T(8,128)(2,1)S(1)}) fusion(f32[6144,256]{1,0:T(8,128)S(1)} %bitcast.137, bf16[6144,256]{1,0:T(8,128)(2,1)S(1)} %get-tuple-element.26, bf16[1,256,256]{2,1,0:T(8,128)(2,1)S(1)} %copy-done), kind=kOutput, calls=%fused_computation.8 | convolution fusion | flops 822607616 | bytes 12715008 | tf_op jit(solution)/shard_map/dot_general | solution.py:121
  80.8 4.5 %collective-permute-start.2 = (f32[1540]{0:T(1024)S(1)}, f32[1540]{0:T(1024)S(1)}, u32[]{:S(2)}, u32[]{:S(2)}) collective-permute-start(f32[1540]{0:T(1024)S(1)} %pad_maximum_fusion.6), channel_id=1, source_target_pairs={{0,1},{1,0},{2,3},{3,2},{4,5},{5,4},{6,7},{7,6},{8,9},{9,8},{10,11... | collective-permute-start | bytes 18488 | tf_op jit(solution)/shard_map/ppermute | solution.py:241
  85.4 1.0 %fusion.12 = f32[256,256]{1,0:T(8,128)S(1)} fusion(bf16[6144,256]{1,0:T(8,128)(2,1)S(1)} %get-tuple-element.28, bf16[6144,128]{1,0:T(8,128)(2,1)S(1)} %copy-done.4, bf16[6144,128]{1,0:T(8,128)(2,1)S(1)} %copy-done.2), kind=kOutput, calls=%fused_computation.39 | convolution fusion | flops 811597824 | bytes 6553600 | tf_op jit(solution)/shard_map/dot_general | solution.py:125
  (102 shorter events, 10.8 us)
Async XLA Ops:
  0.6 30.2 %copy-start = (bf16[1,256,256]{2,1,0:T(8,128)(2,1)S(1)}, bf16[1,256,256]{2,1,0:T(8,128)(2,1)}, u32[]{:S(2)}) copy-start(bf16[1,256,256]{2,1,0:T(8,128)(2,1)} %param.20) | copy-start | bytes 393220
  1.8 24.3 %copy-start.10 = (f32[1,256]{1,0:T(1,128)S(1)}, f32[1,256]{1,0:T(1,128)}, u32[]{:S(2)}) copy-start(f32[1,256]{1,0:T(1,128)} %param.19) | copy-start | bytes 3076
  2.0 17.0 %copy-start.9 = (s32[128]{0:T(128)}, s32[128]{0:T(128)S(1)}, u32[]{:S(2)}) copy-start(s32[128]{0:T(128)S(1)} %multiply_add_fusion.2) | copy-start | bytes 1540
  4.9 14.1 %all-to-all-start = ((f32[16,12,128]{2,1,0:T(8,128)}), f32[16,12,128]{2,1,0:T(8,128)S(1)}, u32[]{:S(2)}, u32[]{:S(2)}) async-start(f32[16,12,128]{2,1,0:T(8,128)} %fusion.21), calls=%async_computation | async-start | bytes 262144 | tf_op jit(solution)/shard_map/all_to_all | solution.py:179
  26.1 4.8 %copy-start.1 = (bf16[6144,128]{1,0:T(8,128)(2,1)}, bf16[6144,128]{1,0:T(8,128)(2,1)S(1)}, u32[]{:S(2)}) copy-start(bf16[6144,128]{1,0:T(8,128)(2,1)S(1)} %get-tuple-element.12) | copy-start | bytes 4718596
  26.1 4.8 %copy-start.3 = (bf16[6144,128]{1,0:T(8,128)(2,1)}, bf16[6144,128]{1,0:T(8,128)(2,1)S(1)}, u32[]{:S(2)}) copy-start(bf16[6144,128]{1,0:T(8,128)(2,1)S(1)} %get-tuple-element.13) | copy-start | bytes 4718596
  26.1 4.8 %copy-start.11 = (f32[1,256]{1,0:T(1,128)S(1)}, f32[1,256]{1,0:T(1,128)}, u32[]{:S(2)}) copy-start(f32[1,256]{1,0:T(1,128)} %param.21) | copy-start | bytes 3076
  30.8 4.4 %copy-start.12 = (bf16[6144,256]{1,0:T(8,128)(2,1)}, bf16[6144,256]{1,0:T(8,128)(2,1)S(1)}, u32[]{:S(2)}) copy-start(bf16[6144,256]{1,0:T(8,128)(2,1)S(1)} %get-tuple-element.21) | copy-start | bytes 9437188
  30.9 4.4 %copy-start.6 = (bf16[1,4,256]{2,1,0:T(4,128)(2,1)S(1)}, bf16[1,4,256]{2,1,0:T(4,128)(2,1)}, u32[]{:S(2)}) copy-start(bf16[1,4,256]{2,1,0:T(4,128)(2,1)} %param.22) | copy-start | bytes 6148
  30.9 4.4 %copy-start.7 = (f32[1,4]{1,0:T(1,128)S(1)}, f32[1,4]{1,0:T(1,128)}, u32[]{:S(2)}) copy-start(f32[1,4]{1,0:T(1,128)} %param.23) | copy-start | bytes 52
  35.3 8.7 %copy-start.8 = (f32[3,16]{1,0:T(4,128)S(1)}, f32[3,16]{1,0:T(4,128)}, u32[]{:S(2)}) copy-start(f32[3,16]{1,0:T(4,128)} %param.16) | copy-start | bytes 580
  35.3 17.6 %copy-start.5 = (s32[16,8]{0,1:T(8,128)S(1)}, s32[16,8]{0,1:T(8,128)}, u32[]{:S(2)}) copy-start(s32[16,8]{0,1:T(8,128)} %param.15) | copy-start | bytes 1540
  40.4 9.7 %all-to-all-start.1 = ((f32[4,16,12]{2,0,1:T(4,128)}), f32[4,16,12]{2,0,1:T(4,128)S(1)}, u32[]{:S(2)}, u32[]{:S(2)}) async-start(f32[4,16,12]{2,0,1:T(4,128)} %copy.61), calls=%async_computation.1 | async-start | bytes 65536 | tf_op jit(solution)/shard_map/all_to_all | solution.py:198
  54.9 9.7 %all-to-all-start.2 = ((f32[4,16,12]{2,0,1:T(4,128)}), f32[4,16,12]{2,0,1:T(4,128)S(1)}, u32[]{:S(2)}, u32[]{:S(2)}) async-start(f32[4,16,12]{2,0,1:T(4,128)} %copy.67), calls=%async_computation.2 | async-start | bytes 65536 | tf_op jit(solution)/shard_map/all_to_all | solution.py:223
  71.0 7.0 %slice-start = ((s8[6291456]{0:T(1024)(128)(4,1)}), s8[4194304]{0:T(1024)(128)(4,1)S(1)}, s32[]{:S(2)}) async-start(s8[6291456]{0:T(1024)(128)(4,1)} %bitcast.136), calls=%async_computation.3 | async-start | bytes 8388608
  71.7 5.2 %copy-start.13 = (bf16[6144,256]{1,0:T(8,128)(2,1)S(1)}, bf16[6144,256]{1,0:T(8,128)(2,1)}, u32[]{:S(2)}) copy-start(bf16[6144,256]{1,0:T(8,128)(2,1)} %copy-done.12) | copy-start | bytes 9437188
  71.7 6.2 %slice-start.1 = ((s8[6291456]{0:T(1024)(128)(4,1)}), s8[2097152]{0:T(1024)(128)(4,1)S(1)}, s32[]{:S(2)}) async-start(s8[6291456]{0:T(1024)(128)(4,1)} %bitcast.136), calls=%async_computation.4 | async-start | bytes 4194304
  78.0 7.4 %copy-start.2 = (bf16[6144,128]{1,0:T(8,128)(2,1)S(1)}, bf16[6144,128]{1,0:T(8,128)(2,1)}, u32[]{:S(2)}) copy-start(bf16[6144,128]{1,0:T(8,128)(2,1)} %copy-done.1) | copy-start | bytes 4718596
  78.0 7.4 %copy-start.4 = (bf16[6144,128]{1,0:T(8,128)(2,1)S(1)}, bf16[6144,128]{1,0:T(8,128)(2,1)}, u32[]{:S(2)}) copy-start(bf16[6144,128]{1,0:T(8,128)(2,1)} %copy-done.3) | copy-start | bytes 4718596
  80.8 6.2 %collective-permute-start.2 = (f32[1540]{0:T(1024)S(1)}, f32[1540]{0:T(1024)S(1)}, u32[]{:S(2)}, u32[]{:S(2)}) collective-permute-start(f32[1540]{0:T(1024)S(1)} %pad_maximum_fusion.6), channel_id=1, source_target_pairs={{0,1},{1,0},{2,3},{3,2},{4,5},{5,4},{6,7},{7,6},{8,9},{9,8},{10,11... | collective-permute-start | bytes 18488 | tf_op jit(solution)/shard_map/ppermute | solution.py:241
  85.3 3.4 %collective-permute-start.1 = (f32[128,256]{1,0:T(8,128)S(1)}, f32[128,256]{1,0:T(8,128)S(1)}, u32[]{:S(2)}, u32[]{:S(2)}) collective-permute-start(f32[128,256]{1,0:T(8,128)S(1)} %constant_dynamic-slice_fusion.1), channel_id=1, source_target_pairs={{0,1},{1,0},{2,3},{3,2},{4,5},{5,4},{6,7},{7,6},{8,9},{9,8},{10,11... | collective-permute-start | bytes 393224 | tf_op jit(solution)/shard_map/ppermute | solution.py:241
  86.4 2.9 %collective-permute-start = (f32[128,256]{1,0:T(8,128)S(1)}, f32[128,256]{1,0:T(8,128)S(1)}, u32[]{:S(2)}, u32[]{:S(2)}) collective-permute-start(f32[128,256]{1,0:T(8,128)S(1)} %constant_dynamic-slice_fusion), channel_id=1, source_target_pairs={{0,1},{1,0},{2,3},{3,2},{4,5},{5,4},{6,7},{7,6},{8,9},{9,8},{10,11... | collective-permute-start | bytes 393224 | tf_op jit(solution)/shard_map/ppermute | solution.py:241
where the time goes:
time: 90.9 us; the launch traced here: 90 us
  matrix products  23.1 us (25%)
  starting transfers between devices  19.7 us (22%)
  local copies, waits for them, and re-layouts  17.7 us (19%)
  waiting for transfers between devices  16.6 us (18%)
  other arithmetic  11.7 us (13%)
  between operations  1.15 us (1%)
    all_to_all x1, starting transfers between devices, per_device(): lax.all_to_all(outgoing, 'space', split_axis=0, concat_axis=0, tiled=True)  7.41 us
    all_to_all x1, waiting for transfers between devices, per_device(): lax.all_to_all(sendback, 'space', split_axis=1, concat_axis=1, tiled=True)  6.02 us
    all_to_all x1, waiting for transfers between devices, per_device(): lax.all_to_all(outgoing, 'space', split_axis=0, concat_axis=0, tiled=True)  5.85 us
    another operation x2, other arithmetic  5.68 us
    dot_general x1, matrix products, backward(): jnp.dot(grad_raw, head_weight, preferred_element_type=jnp.float32)  5.17 us
    ppermute x3, starting transfers between devices, per_device(): lax.ppermute((send_first, send_second, small), 'ray', pairs)  5.1 us
    dot_general x1, matrix products, network(): jnp.dot(encoded, first_weight, preferred_element_type=jnp.float32)  4.73 us
    all_to_all x1, waiting for transfers between devices, per_device(): lax.all_to_all(partials, 'space', split_axis=1, concat_axis=1, tiled=True)  4.71 us
  transfers between devices with their start and end apart: 6, of which 3 were waited for; matrix products, arithmetic and copies ran while one was open for 6% of the time, Pallas kernels for 0%

commit v1 on v0

--- a/solution.py
+++ b/solution.py
@@ -6,6 +6,22 @@
 SEG_LEN = 32
 SEGS = 8
 two_pi = 6.283185307179586
+
+
+def pairwise_exchange(x, axis, split, join):
+    ways, here = (lax.axis_size(axis), lax.axis_index(axis))
+    width = x.shape[split] // ways
+    shape = list(x.shape)
+    shape[split] = width
+    height = shape[join]
+    shape[join] = height * ways
+    full = jnp.zeros(shape, x.dtype)
+    for mask in range(ways):
+        part = lax.dynamic_slice_in_dim(x, (here ^ mask) * width, width, axis=split)
+        if mask:
+            part = lax.ppermute(part, axis, [(d, d ^ mask) for d in range(ways)])
+        full = lax.dynamic_update_slice_in_dim(full, part, (here ^ mask) * height, axis=join)
+    return full
 
 
 def silu_slope(value):
@@ -220,7 +236,7 @@
         preferred_element_type=jnp.float32,
     )
     sendback = sendback.reshape(4, groups, capacity)
-    received = lax.all_to_all(sendback, "space", split_axis=1, concat_axis=1, tiled=True)
+    received = pairwise_exchange(sendback, "space", 1, 1)
     received = received.reshape(4, slot_count).T
     totals = backward(samples, params, saved, received[:, :3], received[:, 3])
     grad_first, grad_second, grad_head, bias_first, bias_second, bias_head = totals

time: 90.9 us -> 121 us (1.33)
  starting transfers between devices: 19.7 us -> 41.9 us
  local copies, waits for them, and re-layouts: 17.7 us -> 29 us
  waiting for transfers between devices: 16.6 us -> 10.4 us
  other arithmetic: 11.7 us -> 13.6 us
    ppermute x0 -> x15, starting transfers between devices: none -> 22.9 us  [pairwise_exchange(): part = lax.ppermute(part, axis, [(d, d ^ mask) for d in range(ways)])]
    dynamic_update_slice x0 -> x16, local copies, waits for them, and re-layouts: none -> 9.72 us  [pairwise_exchange(): lax.dynamic_update_slice_in_dim(full, part, (here ^ mask) * height, axis=...]
    all_to_all x1 -> x0, waiting for transfers between devices: 6.02 us -> none  [per_device(): lax.all_to_all(sendback, 'space', split_axis=1, concat_axis=1, tiled=True)]
    all_to_all x1 -> x0, starting transfers between devices: 3.68 us -> none  [per_device(): lax.all_to_all(sendback, 'space', split_axis=1, concat_axis=1, tiled=True)]
    ppermute x3, starting transfers between devices: 5.1 us -> 8.09 us  [per_device(): lax.ppermute((send_first, send_second, small), 'ray', pairs)]
    unnamed x36 -> x40, local copies, waits for them, and re-layouts: 1.02 us -> 2.6 us
  transfers between devices with their start and end apart: 6 -> 20, of which waited for: 3 -> 2; matrix products, arithmetic and copies ran while one was open for 6% -> 14% of each run, Pallas kernels for 0% -> 0%
where the time goes in v1:
time: 121 us; the launch traced here: 119 us
  starting transfers between devices  41.9 us (35%)
  local copies, waits for them, and re-layouts  29 us (24%)
  matrix products  23.2 us (19%)
  other arithmetic  13.6 us (11%)
  waiting for transfers between devices  10.4 us (9%)
  between operations  1.37 us (1%)
    ppermute x15, starting transfers between devices, pairwise_exchange(): part = lax.ppermute(part, axis, [(d, d ^ mask) for d in range(ways)])  22.9 us
    dynamic_update_slice x16, local copies, waits for them, and re-layouts, pairwise_exchange(): lax.dynamic_update_slice_in_dim(full, part, (here ^ mask) * height, axis=...  9.72 us
    ppermute x3, starting transfers between devices, per_device(): lax.ppermute((send_first, send_second, small), 'ray', pairs)  8.09 us
    all_to_all x1, starting transfers between devices, per_device(): lax.all_to_all(outgoing, 'space', split_axis=0, concat_axis=0, tiled=True)  7.41 us
    all_to_all x1, waiting for transfers between devices, per_device(): lax.all_to_all(outgoing, 'space', split_axis=0, concat_axis=0, tiled=True)  5.84 us
    another operation x2, other arithmetic  5.68 us
    dot_general x1, matrix products, backward(): jnp.dot(grad_raw, head_weight, preferred_element_type=jnp.float32)  5.17 us
    dot_general x1, matrix products, network(): jnp.dot(encoded, first_weight, preferred_element_type=jnp.float32)  4.72 us
  transfers between devices with their start and end apart: 20, of which 2 were waited for; matrix products, arithmetic and copies ran while one was open for 14% of the time, Pallas kernels for 0%

profile of v1, /device:TPU:1, one launch (start us, length us, event | category | flops | bytes accessed | tf_op | source)
XLA Modules:
  0.0 119.5 jit_solution(9917439147552206857)
XLA Ops:
  2.0 0.9 reshape.234
  4.0 0.9 fusion.21
  4.9 7.4 %all-to-all-start = ((f32[16,12,128]{2,1,0:T(8,128)}), f32[16,12,128]{2,1,0:T(8,128)S(1)}, u32[]{:S(2)}, u32[]{:S(2)}) async-start(f32[16,12,128]{2,1,0:T(8,128)} %fusion.21), calls=%async_computation | async-start | bytes 262144 | tf_op jit(solution)/shard_map/all_to_all | solution.py:195
  13.1 5.8 %all-to-all-done = f32[16,12,128]{2,1,0:T(8,128)S(1)} async-done(((f32[16,12,128]{2,1,0:T(8,128)}), f32[16,12,128]{2,1,0:T(8,128)S(1)}, u32[]{:S(2)}, u32[]{:S(2)}) %all-to-all-start) | async-done | bytes 98336 | tf_op jit(solution)/shard_map/all_to_all | solution.py:195
  19.2 0.9 slice_reduce_fusion.2
  20.4 5.6 %fusion.2 = (bf16[6144,128]{1,0:T(8,128)(2,1)S(1)}, bf16[6144,128]{1,0:T(8,128)(2,1)S(1)}) fusion(f32[128]{0:T(128)S(1)} %get-tuple-element.35, f32[6144]{0:T(1024)S(1)} %mul.319, f32[128]{0:T(128)S(1)} %get-tuple-element.36, f32[6144]{0:T(1024)S(1)} %mul.314, f32[128]{0:T(128)S(1)} %get-tuple-element.34, f32[6144]{0:T(1024)S(1)} %mul.309), kind=kLoop, calls=%fused_computation.15 | loop fusion | flops 36175872 | bytes 3220992 | tf_op jit(solution)/shard_map/convert.4
  26.1 4.7 %multiply_convert_fusion.1 = (bf16[6144,256]{1,0:T(8,128)(2,1)S(1)}, f32[6144,256]{1,0:T(8,128)}) fusion(f32[256]{0:T(256)S(1)} %bitcast.134, bf16[1,256,256]{2,1,0:T(8,128)(2,1)} %param.18, bf16[6144,128]{1,0:T(8,128)(2,1)S(1)} %get-tuple-element.13, bf16[6144,128]{1,0:T(8,128)(2,1)S(1)} %get-tuple-element.12), kind=kOutput, calls=%fused_computation.11 | convolution fusion | flops 821035008 | bytes 12715008 | tf_op jit(solution)/shard_map/dot_general | solution.py:77
  30.9 4.4 %multiply_convert_fusion = (bf16[6144,256]{1,0:T(8,128)(2,1)S(1)}, f32[6144,256]{1,0:T(8,128)}) fusion(f32[256]{0:T(256)S(1)} %bitcast.135, bf16[6144,256]{1,0:T(8,128)(2,1)S(1)} %get-tuple-element.37, bf16[1,256,256]{2,1,0:T(8,128)(2,1)S(1)} %copy-done), kind=kOutput, calls=%fused_computation.9 | convolution fusion | flops 814743552 | bytes 12715008 | tf_op jit(solution)/shard_map/dot_general | solution.py:79
  35.3 0.9 convolution_add_fusion.2
  36.2 0.9 reshape.238
  37.1 1.5 %slice.77 = f32[192,32,1]{1,0,2:T(8,128)} slice(f32[192,32,4]{1,0,2:T(8,128)} %reshape.238), slice={[0:192], [0:32], [0:1]} | slice | bytes 49152 | tf_op jit(solution)/shard_map/slice | solution.py:88
  38.7 1.0 copy.72
  39.9 1.2 multiply_reduce_fusion.1
  41.9 3.5 %all-to-all-start.1 = ((f32[4,16,12]{2,0,1:T(4,128)}), f32[4,16,12]{2,0,1:T(4,128)S(1)}, u32[]{:S(2)}, u32[]{:S(2)}) async-start(f32[4,16,12]{2,0,1:T(4,128)} %copy.59), calls=%async_computation.1 | async-start | bytes 65536 | tf_op jit(solution)/shard_map/all_to_all | solution.py:214
  47.1 4.5 %all-to-all-done.1 = f32[4,16,12]{2,0,1:T(4,128)S(1)} async-done(((f32[4,16,12]{2,0,1:T(4,128)}), f32[4,16,12]{2,0,1:T(4,128)S(1)}, u32[]{:S(2)}, u32[]{:S(2)}) %all-to-all-start.1) | async-done | bytes 3104 | tf_op jit(solution)/shard_map/all_to_all | solution.py:214
  57.1 2.1 %collective-permute-start.2 = (f32[4,1,12]{2,1,0:T(1,128)}, f32[4,1,12]{2,1,0:T(1,128)}, u32[]{:S(2)}, u32[]{:S(2)}) collective-permute-start(f32[4,1,12]{2,1,0:T(1,128)} %get-tuple-element.26), channel_id=1, source_target_pairs={{0,6},{2,4},{4,2},{6,0},{8,14},{10,12},{12,10},{14,8},{16,22},{18,... | collective-permute-start | bytes 584 | tf_op jit(solution)/shard_map/ppermute | solution.py:22
  59.5 1.3 %collective-permute-start.4 = (f32[4,1,12]{2,1,0:T(1,128)}, f32[4,1,12]{2,1,0:T(1,128)}, u32[]{:S(2)}, u32[]{:S(2)}) collective-permute-start(f32[4,1,12]{2,1,0:T(1,128)} %get-tuple-element.24), channel_id=1, source_target_pairs={{0,10},{2,8},{4,14},{6,12},{8,2},{10,0},{12,6},{14,4},{16,26},{18,... | collective-permute-start | bytes 584 | tf_op jit(solution)/shard_map/ppermute | solution.py:22
  62.0 2.8 %collective-permute-start.6 = (f32[4,1,12]{2,1,0:T(1,128)}, f32[4,1,12]{2,1,0:T(1,128)}, u32[]{:S(2)}, u32[]{:S(2)}) collective-permute-start(f32[4,1,12]{2,1,0:T(1,128)} %get-tuple-element.22), channel_id=1, source_target_pairs={{0,14},{2,12},{4,10},{6,8},{8,6},{10,4},{12,2},{14,0},{16,30},{18,... | collective-permute-start | bytes 584 | tf_op jit(solution)/shard_map/ppermute | solution.py:22
  66.6 2.2 %collective-permute-start.8 = (f32[4,1,12]{2,1,0:T(1,128)}, f32[4,1,12]{2,1,0:T(1,128)}, u32[]{:S(2)}, u32[]{:S(2)}) collective-permute-start(f32[4,1,12]{2,1,0:T(1,128)} %get-tuple-element.20), channel_id=1, source_target_pairs={{0,18},{2,16},{4,22},{6,20},{8,26},{10,24},{12,30},{14,28},{16,2},... | collective-permute-start | bytes 584 | tf_op jit(solution)/shard_map/ppermute | solution.py:22
  70.7 3.7 %collective-permute-start.10 = (f32[4,1,12]{2,1,0:T(1,128)}, f32[4,1,12]{2,1,0:T(1,128)}, u32[]{:S(2)}, u32[]{:S(2)}) collective-permute-start(f32[4,1,12]{2,1,0:T(1,128)} %get-tuple-element.18), channel_id=1, source_target_pairs={{0,22},{2,20},{4,18},{6,16},{8,30},{10,28},{12,26},{14,24},{16,6},... | collective-permute-start | bytes 584 | tf_op jit(solution)/shard_map/ppermute | solution.py:22
  76.3 2.9 %collective-permute-start.12 = (f32[4,1,12]{2,1,0:T(1,128)}, f32[4,1,12]{2,1,0:T(1,128)}, u32[]{:S(2)}, u32[]{:S(2)}) collective-permute-start(f32[4,1,12]{2,1,0:T(1,128)} %get-tuple-element.16), channel_id=1, source_target_pairs={{0,26},{2,24},{4,30},{6,28},{8,18},{10,16},{12,22},{14,20},{16,10}... | collective-permute-start | bytes 584 | tf_op jit(solution)/shard_map/ppermute | solution.py:22
  81.0 4.7 %collective-permute-start.14 = (f32[4,1,12]{2,1,0:T(1,128)S(1)}, f32[4,1,12]{2,1,0:T(1,128)}, u32[]{:S(2)}, u32[]{:S(2)}) collective-permute-start(f32[4,1,12]{2,1,0:T(1,128)S(1)} %get-tuple-element.14), channel_id=1, source_target_pairs={{0,30},{2,28},{4,26},{6,24},{8,22},{10,20},{12,18},{14,16},{16,14}... | collective-permute-start | bytes 584 | tf_op jit(solution)/shard_map/ppermute | solution.py:22
  89.3 2.4 %multiply_reduce_fusion = (f32[192,32]{1,0:T(8,128)}, bf16[192,32,3]{1,0,2:T(8,128)(2,1)}) fusion(f32[192,3]{0,1:T(4,128)S(1)} %bitcast.126, f32[192,32,4]{1,0,2:T(8,128)} %reshape.238, f32[192,32]{1,0:T(8,128)S(1)} %copy.58), kind=kLoop, calls=%fused_computation.47 | loop fusion | flops 178176 | bytes 162048 | tf_op jit(solution)/shard_map/reduce_sum | solution.py:116
  91.8 1.0 copy.65
  93.1 1.1 concatenate.35
  95.0 5.2 %convert_reduce_fusion = (f32[256]{0:T(256)S(1)}, bf16[6144,256]{1,0:T(8,128)(2,1)S(1)}) fusion(f32[6144,256]{1,0:T(8,128)} %get-tuple-element.40, bf16[1,4,256]{2,1,0:T(4,128)(2,1)S(1)} %copy-done.8, bf16[6144,3]{0,1:T(4,128)(2,1)S(1)} %concatenate.35, bf16[6144,1]{0,1:T(2,128)(2,1)S(1)} %concatenate.34), kind=kOutput, calls=%fused_computation.7 | convolution fusion | flops 29982464 | bytes 9489408 | tf_op jit(solution)/shard_map/dot_general | solution.py:131
  100.2 1.0 fusion.56
  101.3 2.8 %convert_reduce_fusion.1 = (f32[256]{0:T(256)S(1)}, bf16[6144,256]{1,0:T(8,128)(2,1)S(1)}) fusion(f32[6144,256]{1,0:T(8,128)S(1)} %bitcast.137, bf16[6144,256]{1,0:T(8,128)(2,1)S(1)} %get-tuple-element.42, bf16[1,256,256]{2,1,0:T(8,128)(2,1)S(1)} %copy-done), kind=kOutput, calls=%fused_computation.8 | convolution fusion | flops 822607616 | bytes 12715008 | tf_op jit(solution)/shard_map/dot_general | solution.py:137
  104.1 7.5 %collective-permute-start.17 = (f32[1540]{0:T(1024)S(1)}, f32[1540]{0:T(1024)S(1)}, u32[]{:S(2)}, u32[]{:S(2)}) collective-permute-start(f32[1540]{0:T(1024)S(1)} %pad_maximum_fusion.6), channel_id=1, source_target_pairs={{0,1},{1,0},{2,3},{3,2},{4,5},{5,4},{6,7},{7,6},{8,9},{9,8},{10,11... | collective-permute-start | bytes 18488 | tf_op jit(solution)/shard_map/ppermute | solution.py:257
  112.3 1.0 fusion.12
  116.3 1.6 %add_bitcast_fusion = f32[1,128,256]{2,1,0:T(8,128)} fusion(f32[128,256]{1,0:T(8,128)S(1)} %collective-permute-done.16, f32[256,256]{1,0:T(8,128)} %copy-done.5, s32[]{:T(128)S(6)} %select_n.129), kind=kLoop, calls=%fused_computation.52 | loop fusion | flops 32768 | bytes 393220 | tf_op jit(solution)/shard_map/broadcast_in_dim | solution.py:278
  117.9 1.6 %add_bitcast_fusion.1 = f32[1,128,256]{2,1,0:T(8,128)} fusion(f32[128,256]{1,0:T(8,128)S(1)} %collective-permute-done.15, f32[256,256]{1,0:T(8,128)} %copy-done.6, s32[]{:T(128)S(6)} %select_n.129), kind=kLoop, calls=%fused_computation.53 | loop fusion | flops 32768 | bytes 393220 | tf_op jit(solution)/shard_map/broadcast_in_dim | solution.py:277
  (150 shorter events, 29.0 us)
Async XLA Ops:
  0.6 30.2 %copy-start = (bf16[1,256,256]{2,1,0:T(8,128)(2,1)S(1)}, bf16[1,256,256]{2,1,0:T(8,128)(2,1)}, u32[]{:S(2)}) copy-start(bf16[1,256,256]{2,1,0:T(8,128)(2,1)} %param.20) | copy-start | bytes 393220
  1.8 24.3 %copy-start.12 = (f32[1,256]{1,0:T(1,128)S(1)}, f32[1,256]{1,0:T(1,128)}, u32[]{:S(2)}) copy-start(f32[1,256]{1,0:T(1,128)} %param.19) | copy-start | bytes 3076
  2.0 11.1 %copy-start.11 = (s32[128]{0:T(128)}, s32[128]{0:T(128)S(1)}, u32[]{:S(2)}) copy-start(s32[128]{0:T(128)S(1)} %multiply_add_fusion.2) | copy-start | bytes 1540
  4.9 14.1 %all-to-all-start = ((f32[16,12,128]{2,1,0:T(8,128)}), f32[16,12,128]{2,1,0:T(8,128)S(1)}, u32[]{:S(2)}, u32[]{:S(2)}) async-start(f32[16,12,128]{2,1,0:T(8,128)} %fusion.21), calls=%async_computation | async-start | bytes 262144 | tf_op jit(solution)/shard_map/all_to_all | solution.py:195
  26.1 4.8 %copy-start.1 = (bf16[6144,128]{1,0:T(8,128)(2,1)}, bf16[6144,128]{1,0:T(8,128)(2,1)S(1)}, u32[]{:S(2)}) copy-start(bf16[6144,128]{1,0:T(8,128)(2,1)S(1)} %get-tuple-element.12) | copy-start | bytes 4718596
  35.3 10.3 %copy-start.10 = (f32[3,16]{1,0:T(4,128)S(1)}, f32[3,16]{1,0:T(4,128)}, u32[]{:S(2)}) copy-start(f32[3,16]{1,0:T(4,128)} %param.16) | copy-start | bytes 580
  35.3 19.1 %copy-start.7 = (s32[16,8]{0,1:T(8,128)S(1)}, s32[16,8]{0,1:T(8,128)}, u32[]{:S(2)}) copy-start(s32[16,8]{0,1:T(8,128)} %param.15) | copy-start | bytes 1540
  41.9 9.7 %all-to-all-start.1 = ((f32[4,16,12]{2,0,1:T(4,128)}), f32[4,16,12]{2,0,1:T(4,128)S(1)}, u32[]{:S(2)}, u32[]{:S(2)}) async-start(f32[4,16,12]{2,0,1:T(4,128)} %copy.59), calls=%async_computation.1 | async-start | bytes 65536 | tf_op jit(solution)/shard_map/all_to_all | solution.py:214
  56.5 4.3 %collective-permute-start = (f32[4,1,12]{2,1,0:T(1,128)}, f32[4,1,12]{2,1,0:T(1,128)}, u32[]{:S(2)}, u32[]{:S(2)}) collective-permute-start(f32[4,1,12]{2,1,0:T(1,128)} %get-tuple-element.28), channel_id=1, source_target_pairs={{0,2},{2,0},{4,6},{6,4},{8,10},{10,8},{12,14},{14,12},{16,18},{18,... | collective-permute-start | bytes 584 | tf_op jit(solution)/shard_map/ppermute | solution.py:22
  57.0 5.0 %collective-permute-start.1 = (f32[4,1,12]{2,1,0:T(1,128)}, f32[4,1,12]{2,1,0:T(1,128)}, u32[]{:S(2)}, u32[]{:S(2)}) collective-permute-start(f32[4,1,12]{2,1,0:T(1,128)} %get-tuple-element.27), channel_id=1, source_target_pairs={{0,4},{2,6},{4,0},{6,2},{8,12},{10,14},{12,8},{14,10},{16,20},{18,... | collective-permute-start | bytes 584 | tf_op jit(solution)/shard_map/ppermute | solution.py:22
  57.1 8.4 %collective-permute-start.2 = (f32[4,1,12]{2,1,0:T(1,128)}, f32[4,1,12]{2,1,0:T(1,128)}, u32[]{:S(2)}, u32[]{:S(2)}) collective-permute-start(f32[4,1,12]{2,1,0:T(1,128)} %get-tuple-element.26), channel_id=1, source_target_pairs={{0,6},{2,4},{4,2},{6,0},{8,14},{10,12},{12,10},{14,8},{16,22},{18,... | collective-permute-start | bytes 584 | tf_op jit(solution)/shard_map/ppermute | solution.py:22
  59.2 7.4 %collective-permute-start.3 = (f32[4,1,12]{2,1,0:T(1,128)}, f32[4,1,12]{2,1,0:T(1,128)}, u32[]{:S(2)}, u32[]{:S(2)}) collective-permute-start(f32[4,1,12]{2,1,0:T(1,128)} %get-tuple-element.25), channel_id=1, source_target_pairs={{0,8},{2,10},{4,12},{6,14},{8,0},{10,2},{12,4},{14,6},{16,24},{18,... | collective-permute-start | bytes 584 | tf_op jit(solution)/shard_map/ppermute | solution.py:22
  59.5 10.0 %collective-permute-start.4 = (f32[4,1,12]{2,1,0:T(1,128)}, f32[4,1,12]{2,1,0:T(1,128)}, u32[]{:S(2)}, u32[]{:S(2)}) collective-permute-start(f32[4,1,12]{2,1,0:T(1,128)} %get-tuple-element.24), channel_id=1, source_target_pairs={{0,10},{2,8},{4,14},{6,12},{8,2},{10,0},{12,6},{14,4},{16,26},{18,... | collective-permute-start | bytes 584 | tf_op jit(solution)/shard_map/ppermute | solution.py:22
  60.8 9.9 %collective-permute-start.5 = (f32[4,1,12]{2,1,0:T(1,128)}, f32[4,1,12]{2,1,0:T(1,128)}, u32[]{:S(2)}, u32[]{:S(2)}) collective-permute-start(f32[4,1,12]{2,1,0:T(1,128)} %get-tuple-element.23), channel_id=1, source_target_pairs={{0,12},{2,14},{4,8},{6,10},{8,4},{10,6},{12,0},{14,2},{16,28},{18,... | collective-permute-start | bytes 584 | tf_op jit(solution)/shard_map/ppermute | solution.py:22
  62.0 13.1 %collective-permute-start.6 = (f32[4,1,12]{2,1,0:T(1,128)}, f32[4,1,12]{2,1,0:T(1,128)}, u32[]{:S(2)}, u32[]{:S(2)}) collective-permute-start(f32[4,1,12]{2,1,0:T(1,128)} %get-tuple-element.22), channel_id=1, source_target_pairs={{0,14},{2,12},{4,10},{6,8},{8,6},{10,4},{12,2},{14,0},{16,30},{18,... | collective-permute-start | bytes 584 | tf_op jit(solution)/shard_map/ppermute | solution.py:22
  65.5 10.8 %collective-permute-start.7 = (f32[4,1,12]{2,1,0:T(1,128)}, f32[4,1,12]{2,1,0:T(1,128)}, u32[]{:S(2)}, u32[]{:S(2)}) collective-permute-start(f32[4,1,12]{2,1,0:T(1,128)} %get-tuple-element.21), channel_id=1, source_target_pairs={{0,16},{2,18},{4,20},{6,22},{8,24},{10,26},{12,28},{14,30},{16,0},... | collective-permute-start | bytes 584 | tf_op jit(solution)/shard_map/ppermute | solution.py:22
  66.6 13.3 %collective-permute-start.8 = (f32[4,1,12]{2,1,0:T(1,128)}, f32[4,1,12]{2,1,0:T(1,128)}, u32[]{:S(2)}, u32[]{:S(2)}) collective-permute-start(f32[4,1,12]{2,1,0:T(1,128)} %get-tuple-element.20), channel_id=1, source_target_pairs={{0,18},{2,16},{4,22},{6,20},{8,26},{10,24},{12,30},{14,28},{16,2},... | collective-permute-start | bytes 584 | tf_op jit(solution)/shard_map/ppermute | solution.py:22
  69.5 11.5 %collective-permute-start.9 = (f32[4,1,12]{2,1,0:T(1,128)}, f32[4,1,12]{2,1,0:T(1,128)S(1)}, u32[]{:S(2)}, u32[]{:S(2)}) collective-permute-start(f32[4,1,12]{2,1,0:T(1,128)} %get-tuple-element.19), channel_id=1, source_target_pairs={{0,20},{2,22},{4,16},{6,18},{8,28},{10,30},{12,24},{14,26},{16,4},... | collective-permute-start | bytes 584 | tf_op jit(solution)/shard_map/ppermute | solution.py:22
  70.7 15.1 %collective-permute-start.10 = (f32[4,1,12]{2,1,0:T(1,128)}, f32[4,1,12]{2,1,0:T(1,128)}, u32[]{:S(2)}, u32[]{:S(2)}) collective-permute-start(f32[4,1,12]{2,1,0:T(1,128)} %get-tuple-element.18), channel_id=1, source_target_pairs={{0,22},{2,20},{4,18},{6,16},{8,30},{10,28},{12,26},{14,24},{16,6},... | collective-permute-start | bytes 584 | tf_op jit(solution)/shard_map/ppermute | solution.py:22
  75.0 11.4 %collective-permute-start.11 = (f32[4,1,12]{2,1,0:T(1,128)}, f32[4,1,12]{2,1,0:T(1,128)}, u32[]{:S(2)}, u32[]{:S(2)}) collective-permute-start(f32[4,1,12]{2,1,0:T(1,128)} %get-tuple-element.17), channel_id=1, source_target_pairs={{0,24},{2,26},{4,28},{6,30},{8,16},{10,18},{12,20},{14,22},{16,8},... | collective-permute-start | bytes 584 | tf_op jit(solution)/shard_map/ppermute | solution.py:22
  76.3 10.8 %collective-permute-start.12 = (f32[4,1,12]{2,1,0:T(1,128)}, f32[4,1,12]{2,1,0:T(1,128)}, u32[]{:S(2)}, u32[]{:S(2)}) collective-permute-start(f32[4,1,12]{2,1,0:T(1,128)} %get-tuple-element.16), channel_id=1, source_target_pairs={{0,26},{2,24},{4,30},{6,28},{8,18},{10,16},{12,22},{14,20},{16,10}... | collective-permute-start | bytes 584 | tf_op jit(solution)/shard_map/ppermute | solution.py:22
  80.0 7.9 %collective-permute-start.13 = (f32[4,1,12]{2,1,0:T(1,128)S(1)}, f32[4,1,12]{2,1,0:T(1,128)}, u32[]{:S(2)}, u32[]{:S(2)}) collective-permute-start(f32[4,1,12]{2,1,0:T(1,128)S(1)} %get-tuple-element.15), channel_id=1, source_target_pairs={{0,28},{2,30},{4,24},{6,26},{8,20},{10,22},{12,16},{14,18},{16,12}... | collective-permute-start | bytes 584 | tf_op jit(solution)/shard_map/ppermute | solution.py:22
  81.0 7.5 %collective-permute-start.14 = (f32[4,1,12]{2,1,0:T(1,128)S(1)}, f32[4,1,12]{2,1,0:T(1,128)}, u32[]{:S(2)}, u32[]{:S(2)}) collective-permute-start(f32[4,1,12]{2,1,0:T(1,128)S(1)} %get-tuple-element.14), channel_id=1, source_target_pairs={{0,30},{2,28},{4,26},{6,24},{8,22},{10,20},{12,18},{14,16},{16,14}... | collective-permute-start | bytes 584 | tf_op jit(solution)/shard_map/ppermute | solution.py:22
  94.2 7.0 %slice-start = ((s8[6291456]{0:T(1024)(128)(4,1)}), s8[4194304]{0:T(1024)(128)(4,1)S(1)}, s32[]{:S(2)}) async-start(s8[6291456]{0:T(1024)(128)(4,1)} %bitcast.136), calls=%async_computation.2 | async-start | bytes 8388608
  95.0 5.2 %copy-start.15 = (bf16[6144,256]{1,0:T(8,128)(2,1)S(1)}, bf16[6144,256]{1,0:T(8,128)(2,1)}, u32[]{:S(2)}) copy-start(bf16[6144,256]{1,0:T(8,128)(2,1)} %copy-done.14) | copy-start | bytes 9437188
  95.0 6.3 %slice-start.1 = ((s8[6291456]{0:T(1024)(128)(4,1)}), s8[2097152]{0:T(1024)(128)(4,1)S(1)}, s32[]{:S(2)}) async-start(s8[6291456]{0:T(1024)(128)(4,1)} %bitcast.136), calls=%async_computation.3 | async-start | bytes 4194304
  101.2 10.4 %copy-start.5 = (f32[256,256]{1,0:T(8,128)}, f32[256,256]{1,0:T(8,128)S(1)}, u32[]{:S(2)}) copy-start(f32[256,256]{1,0:T(8,128)S(1)} %fusion.56) | copy-start | bytes 786436
  101.2 11.1 %copy-start.2 = (bf16[6144,128]{1,0:T(8,128)(2,1)S(1)}, bf16[6144,128]{1,0:T(8,128)(2,1)}, u32[]{:S(2)}) copy-start(bf16[6144,128]{1,0:T(8,128)(2,1)} %copy-done.1) | copy-start | bytes 4718596
  101.2 11.1 %copy-start.4 = (bf16[6144,128]{1,0:T(8,128)(2,1)S(1)}, bf16[6144,128]{1,0:T(8,128)(2,1)}, u32[]{:S(2)}) copy-start(bf16[6144,128]{1,0:T(8,128)(2,1)} %copy-done.3) | copy-start | bytes 4718596
  104.1 10.5 %collective-permute-start.17 = (f32[1540]{0:T(1024)S(1)}, f32[1540]{0:T(1024)S(1)}, u32[]{:S(2)}, u32[]{:S(2)}) collective-permute-start(f32[1540]{0:T(1024)S(1)} %pad_maximum_fusion.6), channel_id=1, source_target_pairs={{0,1},{1,0},{2,3},{3,2},{4,5},{5,4},{6,7},{7,6},{8,9},{9,8},{10,11... | collective-permute-start | bytes 18488 | tf_op jit(solution)/shard_map/ppermute | solution.py:257
  112.3 4.0 %collective-permute-start.16 = (f32[128,256]{1,0:T(8,128)}, f32[128,256]{1,0:T(8,128)S(1)}, u32[]{:S(2)}, u32[]{:S(2)}) collective-permute-start(f32[128,256]{1,0:T(8,128)} %constant_dynamic-slice_fusion.17), channel_id=1, source_target_pairs={{0,1},{1,0},{2,3},{3,2},{4,5},{5,4},{6,7},{7,6},{8,9},{9,8},{10,11... | collective-permute-start | bytes 393224 | tf_op jit(solution)/shard_map/ppermute | solution.py:257
  114.1 3.8 %collective-permute-start.15 = (f32[128,256]{1,0:T(8,128)S(1)}, f32[128,256]{1,0:T(8,128)S(1)}, u32[]{:S(2)}, u32[]{:S(2)}) collective-permute-start(f32[128,256]{1,0:T(8,128)S(1)} %constant_dynamic-slice_fusion), channel_id=1, source_target_pairs={{0,1},{1,0},{2,3},{3,2},{4,5},{5,4},{6,7},{7,6},{8,9},{9,8},{10,11... | collective-permute-start | bytes 393224 | tf_op jit(solution)/shard_map/ppermute | solution.py:257
  (6 other events, 23.4 us)
